TPU v7x, 512 devices: a whole 4x8x8 slice. The times are simulated.
512 devices in a mesh: row: 16 (over y, x_lo), col: 16 (over z, core), ka: 2 (over x_hi).
Axes of the slice: x: 4 (x_hi: 2, x_lo: 2; x = x_hi * 2 + x_lo), y: 8, z: 8, core: 2. Of those that a mesh axis runs over, the one named last changes fastest.
Arguments:
- pair: bfloat16 [512, 512, 128], P('row', ('col', 'ka')), may hold values from -6 to 6
- pair_mask: int32 [512, 512], P('row', ('col', 'ka')), may hold values from 0 to 1, as said below
- w_in: bfloat16 [2, 128, 512], replicated, may hold values from -0.5 to 0.5
- w_gate: bfloat16 [2, 128, 128], replicated, may hold values from -0.5 to 0.5
- w_out: bfloat16 [2, 128, 128], replicated, may hold values from -0.5 to 0.5
Outputs:
- updated: bfloat16 [512, 512, 128], P('row', ('col', 'ka'))
Inputs may be any that keep to these rules, and one draw needn't show every extreme that they name: pair_mask[i, j] = v[i] v[j] for a per-token 0/1 validity v; within each aligned run of 16 tokens the real tokens come first and there is at least one.
All inputs are finite; a program needn't handle non-finite values.
Results may differ from a plain program's by a relative error of at most 0.014.
Values may be sent and summed in bfloat16 or wider, within the bound.
No kernel may reach another device: no remote copies, remote signals or barrier semaphores. Data moves between devices by JAX's collectives and lax.ppermute only.
A program may use at most 64 MiB of HBM per device.

v0:
```python
import jax
import jax.numpy as jnp
from jax import lax
from jax.sharding import PartitionSpec as P


def layer_norm(value):
    mean = jnp.mean(value, axis=-1, keepdims=True)
    centred = value - mean
    var = jnp.mean(centred * centred, axis=-1, keepdims=True)
    return centred / jnp.sqrt(var + 1e-05)


def prepare(pair, valid, weight_in, weight_gate):
    normed = layer_norm(pair.astype(jnp.float32)).astype(jnp.bfloat16)
    proj = jnp.einsum("ijc,cd->ijd", normed, weight_in, preferred_element_type=jnp.float32)
    width = proj.shape[-1] // 4
    left = (jax.nn.sigmoid(proj[..., :width]) * proj[..., width : 2 * width] * valid).astype(
        jnp.bfloat16
    )
    right = (
        jax.nn.sigmoid(proj[..., 2 * width : 3 * width]) * proj[..., 3 * width :] * valid
    ).astype(jnp.bfloat16)
    gate = jax.nn.sigmoid(
        jnp.einsum("ijc,cd->ijd", normed, weight_gate, preferred_element_type=jnp.float32)
    )
    return (left, right, gate)


def finish(pair, tri, gate, weight_out):
    normed = layer_norm(tri).astype(jnp.bfloat16)
    proj = jnp.einsum("ijc,cd->ijd", normed, weight_out, preferred_element_type=jnp.float32)
    return (pair.astype(jnp.float32) + gate * proj).astype(jnp.bfloat16)


def transpose_tiles(value, n):
    perm = [(r * n + c, c * n + r) for r in range(n) for c in range(n)]
    return lax.ppermute(value, ("row", "col"), perm)


def gather_a2a(value, axis_name, n, axis):
    copies = jnp.broadcast_to(value[None], (n,) + value.shape)
    got = lax.all_to_all(copies, axis_name, 0, 0, tiled=False)
    got = jnp.moveaxis(got, 0, axis)
    return got.reshape(value.shape[:axis] + (n * value.shape[axis],) + value.shape[axis + 1 :])


def sum_over_ka(partial_value):
    half = partial_value.shape[1] // 2
    me = lax.axis_index("ka")
    mine = lax.dynamic_slice_in_dim(partial_value, me * half, half, axis=1)
    theirs = lax.dynamic_slice_in_dim(partial_value, (1 - me) * half, half, axis=1)
    got = lax.ppermute(theirs.astype(jnp.bfloat16), "ka", [(0, 1), (1, 0)])
    return mine + got.astype(jnp.float32)


def join_over_ka(value):
    me = lax.axis_index("ka")
    got = lax.ppermute(value, "ka", [(0, 1), (1, 0)])
    return jnp.where(
        me == 0, jnp.concatenate([value, got], axis=1), jnp.concatenate([got, value], axis=1)
    )


def on_device(n, pair, pair_mask, w_in, w_gate, w_out):
    valid = pair_mask.astype(jnp.float32)[..., None]
    left, right, gate = prepare(pair, valid, w_in[0], w_gate[0])
    left_rows = lax.all_gather(jnp.swapaxes(left, 0, 1), "col", axis=0, tiled=True)
    right_diag = gather_a2a(jnp.swapaxes(transpose_tiles(right, n), 0, 1), "row", n, 0)
    half = right_diag.shape[1] // 2
    me = lax.axis_index("ka")
    theirs = lax.dynamic_slice_in_dim(right_diag, (1 - me) * half, half, axis=1)
    mine = lax.dynamic_slice_in_dim(right_diag, me * half, half, axis=1)
    sent = jnp.sum(
        left_rows[:, :, None].astype(jnp.float32) * theirs[:, None].astype(jnp.float32), axis=0
    ).astype(jnp.bfloat16)
    sent, left_later, mine = lax.optimization_barrier((sent, left_rows, mine))
    got = lax.ppermute(sent, "ka", [(0, 1), (1, 0)])
    kept = jnp.sum(
        left_later[:, :, None].astype(jnp.float32) * mine[:, None].astype(jnp.float32), axis=0
    )
    tri = kept + got.astype(jnp.float32)
    middle = finish(pair, tri, gate, w_out[0])
    left, right, gate = prepare(middle, valid, w_in[1], w_gate[1])
    right_cols = gather_a2a(right, "row", n, 0)
    left_tile = join_over_ka(transpose_tiles(left, n))
    left_diag = lax.all_gather(left_tile, "col", axis=0, tiled=True)
    tri = jnp.sum(left_diag[:, :, None] * right_cols[:, None], axis=0, dtype=jnp.float32)
    return finish(middle, tri, gate, w_out[1])


def solution(mesh):
    n = mesh.shape["row"]
    assert mesh.shape["col"] == n
    placed = (P("row", ("col", "ka"), None), P("row", ("col", "ka")), P(), P(), P())
    return jax.shard_map(
        lambda *a: on_device(n, *a),
        mesh=mesh,
        in_specs=placed,
        out_specs=P("row", ("col", "ka"), None),
        check_vma=False,
    )
```

profile of v0, /device:TPU:4, one launch (start us, length us, event | category | flops | bytes accessed | tf_op | source)
XLA Modules:
  0.0 218.7 jit_solution(2915067116465360204)
XLA Ops:
  6.5 0.0 all-gather.3.cloned.1.call-start
  6.5 1.0 convert_reduce_fusion.2
  7.6 1.1 fusion.13
  8.8 0.7 convert_element_type.68
  9.5 0.1 copy.14
  9.5 1.3 fusion.37
  10.9 0.0 copy-start.2
  10.9 0.0 copy-start.4
  10.9 0.8 fusion.45
  11.7 0.7 collective-permute-start
  12.4 0.0 all-gather.3.cloned.1.call-update
  12.4 0.0 collective-permute-done
  12.5 1.8 broadcast_in_dim.4
  14.2 26.5 %all-to-all-start = ((bf16[16,16,32,128]{3,2,1,0:T(8,128)(2,1)}), bf16[16,16,32,128]{3,2,1,0:T(8,128)(2,1)S(1)}, u32[]{:S(2)}, u32[]{:S(2)}) async-start(bf16[16,16,32,128]{3,2,1,0:T(8,128)(2,1)} %broadcast_in_dim.4), calls=%async_computation | async-start | bytes 4194304 | tf_op jit(solution)/shard_map/all_to_all | solution.py:43
  40.8 0.0 all-gather.5.cloned.1.call-start
  40.8 0.0 copy-done.2
  40.8 0.0 copy-done.4
  40.8 0.3 fusion.7
  41.2 24.9 %all-gather.3.cloned.1.call-done = bf16[256,32,128]{2,0,1:T(8,128)(2,1)} async-done(((bf16[16,32,128]{2,0,1:T(8,128)(2,1)}), bf16[256,32,128]{2,0,1:T(8,128)(2,1)}) %all-gather.3.cloned.1.call-update) | async-done | bytes 2097168 | tf_op jit(solution)/shard_map/all_gather | solution.py:68
  66.1 4.7 %copy.15 = f32[256,32,128]{2,1,0:T(8,128)} copy(bf16[256,32,128]{2,0,1:T(8,128)(2,1)} %all-gather.3.cloned.1.call-done) | data formatting | bytes 6291456 | tf_op jit(solution)/shard_map/convert_element_type | solution.py:75
  70.8 20.6 %all-to-all-done = bf16[16,16,32,128]{3,2,1,0:T(8,128)(2,1)S(1)} async-done(((bf16[16,16,32,128]{3,2,1,0:T(8,128)(2,1)}), bf16[16,16,32,128]{3,2,1,0:T(8,128)(2,1)S(1)}, u32[]{:S(2)}, u32[]{:S(2)}) %all-to-all-start) | async-done | bytes 2097184 | tf_op jit(solution)/shard_map/all_to_all | solution.py:43
  91.4 0.0 copy-start
  91.4 0.3 constant_dynamic-slice_fusion
  91.7 0.0 copy-start.1
  91.7 1.9 copy-done
  93.6 5.6 %multiply_reduce_fusion.1 = bf16[32,16,128]{2,1,0:T(8,128)(2,1)S(1)} fusion(f32[256,16,128]{2,1,0:T(8,128)S(1)} %get-tuple-element.14, f32[256,32,128]{2,1,0:T(8,128)S(1)} %copy-done), kind=kLoop, calls=%fused_computation.3 | loop fusion | flops 33488896 | bytes 6422528 | tf_op jit(solution)/shard_map/reduce_sum | solution.py:74
  99.2 0.0 copy-done.1
  99.2 1.2 copy.17
  100.5 0.2 convert_element_type.75
  100.6 0.0 copy-start.5
  100.6 0.0 copy-start.3
  100.6 3.0 %collective-permute-start.1 = (bf16[32,16,128]{2,1,0:T(8,128)(2,1)S(1)}, bf16[32,16,128]{2,1,0:T(8,128)(2,1)S(1)}, u32[]{:S(2)}, u32[]{:S(2)}) collective-permute-start(bf16[32,16,128]{2,1,0:T(8,128)(2,1)S(1)} %multiply_reduce_fusion.1), channel_id=1, source_target_pairs={{0,1},{1,0},{2,3},{3,2},{4,5},{5,4},{6,7},{7,6},{8,9},{9,8},{10,11... | collective-permute-start | bytes 393224 | tf_op jit(solution)/shard_map/ppermute | solution.py:78
  103.6 5.6 %multiply_reduce_fusion = f32[32,16,128]{2,1,0:T(8,128)S(1)} fusion(f32[256,16,128]{2,1,0:T(8,128)S(1)} %convert_element_type.75, f32[256,32,128]{2,1,0:T(8,128)S(1)} %copy.17), kind=kLoop, calls=%fused_computation.2 | loop fusion | flops 33488896 | bytes 6553600 | tf_op jit(solution)/shard_map/reduce_sum | solution.py:79
  109.3 0.0 collective-permute-done.1
  109.3 0.1 fusion.46
  109.4 0.2 multiply_reduce_fusion.4
  109.7 0.0 copy-done.5
  109.7 0.4 fusion.57
  110.1 0.2 multiply_reduce_fusion.3
  110.4 0.0 copy-done.3
  110.4 0.4 fusion.35
  110.8 0.2 fusion.21
  110.9 0.7 collective-permute-start.2
  111.6 0.0 collective-permute-done.2
  111.6 4.5 %collective-permute-start.3 = (bf16[32,16,128]{2,1,0:T(8,128)(2,1)S(1)}, bf16[32,16,128]{2,1,0:T(8,128)(2,1)S(1)}, u32[]{:S(2)}, u32[]{:S(2)}) collective-permute-start(bf16[32,16,128]{2,1,0:T(8,128)(2,1)S(1)} %collective-permute-done.2), channel_id=1, source_target_pairs={{0,1},{1,0},{2,3},{3,2},{4,5},{5,4},{6,7},{7,6},{8,9},{9,8},{10,11... | collective-permute-start | bytes 393224 | tf_op jit(solution)/shard_map/ppermute | solution.py:59
  116.1 3.8 %collective-permute-done.3 = bf16[32,16,128]{2,1,0:T(8,128)(2,1)S(1)} collective-permute-done((bf16[32,16,128]{2,1,0:T(8,128)(2,1)S(1)}, bf16[32,16,128]{2,1,0:T(8,128)(2,1)S(1)}, u32[]{:S(2)}, u32[]{:S(2)}) %collective-permute-start.3) | collective-permute-done | bytes 131104 | tf_op jit(solution)/shard_map/ppermute | solution.py:59
  120.0 0.8 maximum_select_fusion
  120.8 0.0 all-gather.5.cloned.1.call-update
  120.8 1.7 broadcast_in_dim.5
  122.6 23.4 %all-to-all-start.1 = ((bf16[16,32,16,128]{3,2,1,0:T(8,128)(2,1)}), bf16[16,32,16,128]{3,2,1,0:T(8,128)(2,1)S(1)}, u32[]{:S(2)}, u32[]{:S(2)}) async-start(bf16[16,32,16,128]{3,2,1,0:T(8,128)(2,1)} %broadcast_in_dim.5), calls=%async_computation.1 | async-start | bytes 4194304 | tf_op jit(solution)/shard_map/all_to_all | solution.py:43
  146.0 0.3 fusion.4
  146.3 48.9 %all-to-all-done.1 = bf16[16,32,16,128]{3,2,1,0:T(8,128)(2,1)S(1)} async-done(((bf16[16,32,16,128]{3,2,1,0:T(8,128)(2,1)}), bf16[16,32,16,128]{3,2,1,0:T(8,128)(2,1)S(1)}, u32[]{:S(2)}, u32[]{:S(2)}) %all-to-all-start.1) | async-done | bytes 2097184 | tf_op jit(solution)/shard_map/all_to_all | solution.py:43
  195.2 0.0 all-gather.5.cloned.1.call-done
  195.2 15.3 %convert_reduce_fusion = (f32[32,16]{1,0:T(8,128)S(1)}, f32[32,16,128]{2,1,0:T(8,128)S(1)}) fusion(bf16[512,16,128]{2,1,0:T(8,128)(2,1)S(1)} %bitcast.31, bf16[512,32,128]{2,1,0:T(8,128)(2,1)} %all-gather.5.cloned.1.call-done), kind=kLoop, calls=%fused_computation | loop fusion | flops 134151680 | bytes 6555648 | tf_op jit(solution)/shard_map/reduce_sum | solution.py:8
  210.6 0.2 multiply_reduce_fusion.2
  210.8 1.0 fusion.10
  (9 shorter events, 0.1 us)
Async XLA Ops:
  6.5 59.5 %all-gather.3.cloned.1.call-start = ((), (), s32[]{:S(2)}) async-start(), calls=%async_computation.2 | async-start | bytes 2228224 | tf_op jit(solution)/shard_map/all_gather | solution.py:68
  10.9 29.9 %copy-start.2 = (bf16[32,16,128]{2,1,0:T(8,128)(2,1)S(1)}, bf16[32,16,128]{2,1,0:T(8,128)(2,1)}, u32[]{:S(2)}) copy-start(bf16[32,16,128]{2,1,0:T(8,128)(2,1)} %param.5) | copy-start | bytes 393220
  10.9 29.9 %copy-start.4 = (bf16[2,128,128]{2,1,0:T(8,128)(2,1)S(1)}, bf16[2,128,128]{2,1,0:T(8,128)(2,1)}, u32[]{:S(2)}) copy-start(bf16[2,128,128]{2,1,0:T(8,128)(2,1)} %param.8) | copy-start | bytes 196612
  11.7 0.7 collective-permute-start
  14.2 77.2 %all-to-all-start = ((bf16[16,16,32,128]{3,2,1,0:T(8,128)(2,1)}), bf16[16,16,32,128]{3,2,1,0:T(8,128)(2,1)S(1)}, u32[]{:S(2)}, u32[]{:S(2)}) async-start(bf16[16,16,32,128]{3,2,1,0:T(8,128)(2,1)} %broadcast_in_dim.4), calls=%async_computation | async-start | bytes 4194304 | tf_op jit(solution)/shard_map/all_to_all | solution.py:43
  40.8 154.5 %all-gather.5.cloned.1.call-start = ((), (), s32[]{:S(2)}) async-start(), calls=%async_computation.3 | async-start | bytes 4456448 | tf_op jit(solution)/shard_map/all_gather | solution.py:87
  91.4 2.2 %copy-start = (f32[256,32,128]{2,1,0:T(8,128)S(1)}, f32[256,32,128]{2,1,0:T(8,128)}, u32[]{:S(2)}) copy-start(f32[256,32,128]{2,1,0:T(8,128)} %copy.15) | copy-start | bytes 12582916
  91.7 7.5 %copy-start.1 = (bf16[256,32,128]{2,0,1:T(8,128)(2,1)S(1)}, bf16[256,32,128]{2,0,1:T(8,128)(2,1)}, u32[]{:S(2)}) copy-start(bf16[256,32,128]{2,0,1:T(8,128)(2,1)} %all-gather.3.cloned.1.call-done) | copy-start | bytes 6291460
  100.6 9.1 %copy-start.5 = (bf16[2,128,128]{2,1,0:T(8,128)(2,1)S(1)}, bf16[2,128,128]{2,1,0:T(8,128)(2,1)}, u32[]{:S(2)}) copy-start(bf16[2,128,128]{2,1,0:T(8,128)(2,1)} %param.9) | copy-start | bytes 196612
  100.6 9.8 %copy-start.3 = (bf16[2,128,512]{2,1,0:T(8,128)(2,1)S(1)}, bf16[2,128,512]{2,1,0:T(8,128)(2,1)}, u32[]{:S(2)}) copy-start(bf16[2,128,512]{2,1,0:T(8,128)(2,1)} %param.7) | copy-start | bytes 786436
  100.6 8.6 %collective-permute-start.1 = (bf16[32,16,128]{2,1,0:T(8,128)(2,1)S(1)}, bf16[32,16,128]{2,1,0:T(8,128)(2,1)S(1)}, u32[]{:S(2)}, u32[]{:S(2)}) collective-permute-start(bf16[32,16,128]{2,1,0:T(8,128)(2,1)S(1)} %multiply_reduce_fusion.1), channel_id=1, source_target_pairs={{0,1},{1,0},{2,3},{3,2},{4,5},{5,4},{6,7},{7,6},{8,9},{9,8},{10,11... | collective-permute-start | bytes 393224 | tf_op jit(solution)/shard_map/ppermute | solution.py:78
  110.9 0.7 collective-permute-start.2
  111.6 8.4 %collective-permute-start.3 = (bf16[32,16,128]{2,1,0:T(8,128)(2,1)S(1)}, bf16[32,16,128]{2,1,0:T(8,128)(2,1)S(1)}, u32[]{:S(2)}, u32[]{:S(2)}) collective-permute-start(bf16[32,16,128]{2,1,0:T(8,128)(2,1)S(1)} %collective-permute-done.2), channel_id=1, source_target_pairs={{0,1},{1,0},{2,3},{3,2},{4,5},{5,4},{6,7},{7,6},{8,9},{9,8},{10,11... | collective-permute-start | bytes 393224 | tf_op jit(solution)/shard_map/ppermute | solution.py:59
  122.6 72.6 %all-to-all-start.1 = ((bf16[16,32,16,128]{3,2,1,0:T(8,128)(2,1)}), bf16[16,32,16,128]{3,2,1,0:T(8,128)(2,1)S(1)}, u32[]{:S(2)}, u32[]{:S(2)}) async-start(bf16[16,32,16,128]{3,2,1,0:T(8,128)(2,1)} %broadcast_in_dim.5), calls=%async_computation.1 | async-start | bytes 4194304 | tf_op jit(solution)/shard_map/all_to_all | solution.py:43
Sparse Core Ops, SparseCore 0:
  12.5 53.4 all-gather.2
  121.0 62.3 all-gather.4
where the time goes:
time: 219 us
  waiting for transfers between devices  98.3 us (45%)
  starting transfers between devices  58.8 us (27%)
  other arithmetic  32.7 us (15%)
  between operations  13.8 us (6%)
  local copies, waits for them, and re-layouts  11.5 us (5%)
  matrix products  3.73 us (2%)
    all_to_all x2, waiting for transfers between devices, gather_a2a(): got = lax.all_to_all(copies, axis_name, 0, 0, tiled=False)  69.5 us
    all_to_all x2, starting transfers between devices, gather_a2a(): got = lax.all_to_all(copies, axis_name, 0, 0, tiled=False)  49.9 us
    all_gather x1, waiting for transfers between devices, on_device(): lax.all_gather(jnp.swapaxes(left, 0, 1), 'col', axis=0, tiled=True)  24.9 us
    reduce_sum x3, other arithmetic, layer_norm(): mean = jnp.mean(value, axis=-1, keepdims=True)  16.5 us
    reduce_sum x1, other arithmetic, on_device(): jnp.sum(left_rows[:, :, None].astype(jnp.float32) * theirs[:, None].astyp...  5.63 us
    reduce_sum x1, other arithmetic, on_device(): jnp.sum(left_later[:, :, None].astype(jnp.float32) * mine[:, None].astype...  5.62 us
    convert_element_type x1, local copies, waits for them, and re-layouts, on_device(): left_rows[:, :, None].astype(jnp.float32)  4.73 us
    ppermute x1, starting transfers between devices, join_over_ka(): got = lax.ppermute(value, 'ka', [(0, 1), (1, 0)])  4.5 us
  transfers between devices with their start and end apart: 8, of which 4 were waited for; matrix products, arithmetic and copies ran while one was open for 7% of the time, Pallas kernels for 0%

commit v1 on v0

--- a/solution.py
+++ b/solution.py
@@ -65,7 +65,14 @@
 def on_device(n, pair, pair_mask, w_in, w_gate, w_out):
     valid = pair_mask.astype(jnp.float32)[..., None]
     left, right, gate = prepare(pair, valid, w_in[0], w_gate[0])
-    left_rows = lax.all_gather(jnp.swapaxes(left, 0, 1), "col", axis=0, tiled=True)
+    in_array = jnp.swapaxes(left, 0, 1)
+    tmp = lax.all_to_all(
+        jnp.stack([in_array] * lax.axis_size("col"), axis=0),
+        axis_name="col",
+        split_axis=0,
+        concat_axis=0,
+    )
+    left_rows = jnp.concatenate(tmp, axis=0)
     right_diag = gather_a2a(jnp.swapaxes(transpose_tiles(right, n), 0, 1), "row", n, 0)
     half = right_diag.shape[1] // 2
     me = lax.axis_index("ka")

time: 219 us -> 270 us (1.23)
  the two profiles are of different devices: /device:TPU:4 before, /device:TPU:1 now
where the time goes in v1:
time: 270 us; the launch traced here: 269 us
  waiting for transfers between devices  159 us (59%)
  starting transfers between devices  49.9 us (18%)
  other arithmetic  36.9 us (14%)
  between operations  13.7 us (5%)
  local copies, waits for them, and re-layouts  6.27 us (2%)
  matrix products  3.72 us (1%)
    all_to_all x2, waiting for transfers between devices, gather_a2a(): got = lax.all_to_all(copies, axis_name, 0, 0, tiled=False)  95.8 us
    all_to_all x1, waiting for transfers between devices, on_device(): lax.all_to_all(jnp.stack([in_array] * lax.axis_size('col'), axis=0), axis...  50.1 us
    all_to_all x2, starting transfers between devices, gather_a2a(): got = lax.all_to_all(copies, axis_name, 0, 0, tiled=False)  25.2 us
    reduce_sum x3, other arithmetic, layer_norm(): mean = jnp.mean(value, axis=-1, keepdims=True)  16.5 us
    all_to_all x1, starting transfers between devices, on_device(): lax.all_to_all(jnp.stack([in_array] * lax.axis_size('col'), axis=0), axis...  11.8 us
    ppermute x2, waiting for transfers between devices, transpose_tiles(): return lax.ppermute(value, ('row', 'col'), perm)  7.89 us
    ppermute x2, starting transfers between devices, transpose_tiles(): return lax.ppermute(value, ('row', 'col'), perm)  6.28 us
    reduce_sum x1, other arithmetic, on_device(): jnp.sum(left_rows[:, :, None].astype(jnp.float32) * theirs[:, None].astyp...  5.63 us
  transfers between devices with their start and end apart: 8, of which 6 were waited for; matrix products, arithmetic and copies ran while one was open for 4% of the time, Pallas kernels for 0%

profile of v1, /device:TPU:1, one launch (start us, length us, event | category | flops | bytes accessed | tf_op | source)
XLA Modules:
  0.0 269.4 jit_solution(12537263196203160141)
XLA Ops:
  6.5 1.0 convert_reduce_fusion.2
  7.6 1.1 fusion.13
  8.8 0.7 convert_element_type.72
  9.5 0.1 copy.12
  9.5 1.3 fusion.37
  10.9 0.2 fusion.45
  11.1 1.8 stack.2
  12.8 11.8 %all-to-all-start = ((bf16[16,16,32,128]{3,2,1,0:T(8,128)(2,1)}), bf16[16,16,32,128]{3,2,1,0:T(8,128)(2,1)S(1)}, u32[]{:S(2)}, u32[]{:S(2)}) async-start(bf16[16,16,32,128]{3,2,1,0:T(8,128)(2,1)} %stack.2), calls=%async_computation | async-start | bytes 4194304 | tf_op jit(solution)/shard_map/all_to_all | solution.py:69
  24.7 0.0 copy-start.1
  24.7 0.0 copy-start.3
  24.7 3.3 %collective-permute-start = (bf16[32,16,128]{2,1,0:T(8,128)(2,1)S(1)}, bf16[32,16,128]{2,1,0:T(8,128)(2,1)S(1)}, u32[]{:S(2)}, u32[]{:S(2)}) collective-permute-start(bf16[32,16,128]{2,1,0:T(8,128)(2,1)S(1)} %get-tuple-element.18), channel_id=1, source_target_pairs={{0,0},{2,32},{4,64},{6,96},{8,128},{10,160},{12,192},{14,224},{16,... | collective-permute-start | bytes 393224 | tf_op jit(solution)/shard_map/ppermute | solution.py:38
  27.9 3.5 %collective-permute-done = bf16[32,16,128]{2,1,0:T(8,128)(2,1)S(1)} collective-permute-done((bf16[32,16,128]{2,1,0:T(8,128)(2,1)S(1)}, bf16[32,16,128]{2,1,0:T(8,128)(2,1)S(1)}, u32[]{:S(2)}, u32[]{:S(2)}) %collective-permute-start) | collective-permute-done | bytes 131104 | tf_op jit(solution)/shard_map/ppermute | solution.py:38
  31.4 50.1 %all-to-all-done = bf16[16,16,32,128]{3,2,1,0:T(8,128)(2,1)S(1)} async-done(((bf16[16,16,32,128]{3,2,1,0:T(8,128)(2,1)}), bf16[16,16,32,128]{3,2,1,0:T(8,128)(2,1)S(1)}, u32[]{:S(2)}, u32[]{:S(2)}) %all-to-all-start) | async-done | bytes 2097184 | tf_op jit(solution)/shard_map/all_to_all | solution.py:69
  81.6 1.7 broadcast_in_dim.4
  83.3 11.4 %all-to-all-start.1 = ((bf16[16,16,32,128]{3,2,1,0:T(8,128)(2,1)}), bf16[16,16,32,128]{3,2,1,0:T(8,128)(2,1)}, u32[]{:S(2)}, u32[]{:S(2)}) async-start(bf16[16,16,32,128]{3,2,1,0:T(8,128)(2,1)} %broadcast_in_dim.4), calls=%async_computation.1 | async-start | bytes 4194304 | tf_op jit(solution)/shard_map/all_to_all | solution.py:43
  94.7 0.0 all-gather.2.cloned.1.call-start
  94.8 0.0 copy-done.1
  94.8 0.0 copy-done.3
  94.8 0.3 fusion.7
  95.1 2.7 bitcast_convert_fusion
  97.8 47.2 %all-to-all-done.1 = bf16[16,16,32,128]{3,2,1,0:T(8,128)(2,1)} async-done(((bf16[16,16,32,128]{3,2,1,0:T(8,128)(2,1)}), bf16[16,16,32,128]{3,2,1,0:T(8,128)(2,1)}, u32[]{:S(2)}, u32[]{:S(2)}) %all-to-all-start.1) | async-done | bytes 2097184 | tf_op jit(solution)/shard_map/all_to_all | solution.py:43
  145.0 0.0 copy-start
  145.0 2.0 constant_dynamic-slice_fusion
  147.0 0.9 copy-done
  147.9 5.6 %multiply_reduce_fusion.1 = bf16[32,16,128]{2,1,0:T(8,128)(2,1)S(1)} fusion(f32[256,16,128]{2,1,0:T(8,128)S(1)} %get-tuple-element.14, f32[256,32,128]{2,1,0:T(8,128)S(1)} %copy-done), kind=kLoop, calls=%fused_computation.3 | loop fusion | flops 33488896 | bytes 6422528 | tf_op jit(solution)/shard_map/reduce_sum | solution.py:81
  153.5 0.6 convert_element_type.78
  154.1 0.2 convert_element_type.79
  154.2 0.0 copy-start.4
  154.3 0.0 copy-start.2
  154.3 4.5 %collective-permute-start.1 = (bf16[32,16,128]{2,1,0:T(8,128)(2,1)S(1)}, bf16[32,16,128]{2,1,0:T(8,128)(2,1)S(1)}, u32[]{:S(2)}, u32[]{:S(2)}) collective-permute-start(bf16[32,16,128]{2,1,0:T(8,128)(2,1)S(1)} %multiply_reduce_fusion.1), channel_id=1, source_target_pairs={{0,1},{1,0},{2,3},{3,2},{4,5},{5,4},{6,7},{7,6},{8,9},{9,8},{10,11... | collective-permute-start | bytes 393224 | tf_op jit(solution)/shard_map/ppermute | solution.py:85
  158.8 5.6 %multiply_reduce_fusion = f32[32,16,128]{2,1,0:T(8,128)S(1)} fusion(f32[256,16,128]{2,1,0:T(8,128)S(1)} %convert_element_type.79, f32[256,32,128]{2,1,0:T(8,128)S(1)} %convert_element_type.78), kind=kLoop, calls=%fused_computation.2 | loop fusion | flops 33488896 | bytes 6553600 | tf_op jit(solution)/shard_map/reduce_sum | solution.py:86
  164.4 0.0 collective-permute-done.1
  164.4 0.1 fusion.46
  164.6 0.2 multiply_reduce_fusion.4
  164.8 0.0 copy-done.4
  164.8 0.4 fusion.57
  165.3 0.2 multiply_reduce_fusion.3
  165.5 0.0 copy-done.2
  165.5 0.4 fusion.35
  165.9 0.2 fusion.21
  166.1 3.0 %collective-permute-start.2 = (bf16[32,16,128]{2,1,0:T(8,128)(2,1)S(1)}, bf16[32,16,128]{2,1,0:T(8,128)(2,1)S(1)}, u32[]{:S(2)}, u32[]{:S(2)}) collective-permute-start(bf16[32,16,128]{2,1,0:T(8,128)(2,1)S(1)} %get-tuple-element.15), channel_id=1, source_target_pairs={{0,0},{2,32},{4,64},{6,96},{8,128},{10,160},{12,192},{14,224},{16,... | collective-permute-start | bytes 393224 | tf_op jit(solution)/shard_map/ppermute | solution.py:38
  169.1 4.4 %collective-permute-done.2 = bf16[32,16,128]{2,1,0:T(8,128)(2,1)S(1)} collective-permute-done((bf16[32,16,128]{2,1,0:T(8,128)(2,1)S(1)}, bf16[32,16,128]{2,1,0:T(8,128)(2,1)S(1)}, u32[]{:S(2)}, u32[]{:S(2)}) %collective-permute-start.2) | collective-permute-done | bytes 131104 | tf_op jit(solution)/shard_map/ppermute | solution.py:38
  173.5 2.1 collective-permute-start.3
  175.7 5.1 %collective-permute-done.3 = bf16[32,16,128]{2,1,0:T(8,128)(2,1)S(1)} collective-permute-done((bf16[32,16,128]{2,1,0:T(8,128)(2,1)S(1)}, bf16[32,16,128]{2,1,0:T(8,128)(2,1)S(1)}, u32[]{:S(2)}, u32[]{:S(2)}) %collective-permute-start.3) | collective-permute-done | bytes 131104 | tf_op jit(solution)/shard_map/ppermute | solution.py:59
  180.7 0.8 maximum_select_fusion
  181.6 0.0 all-gather.2.cloned.1.call-update
  181.6 1.7 broadcast_in_dim.5
  183.3 13.8 %all-to-all-start.2 = ((bf16[16,32,16,128]{3,2,1,0:T(8,128)(2,1)}), bf16[16,32,16,128]{3,2,1,0:T(8,128)(2,1)S(1)}, u32[]{:S(2)}, u32[]{:S(2)}) async-start(bf16[16,32,16,128]{3,2,1,0:T(8,128)(2,1)} %broadcast_in_dim.5), calls=%async_computation.2 | async-start | bytes 4194304 | tf_op jit(solution)/shard_map/all_to_all | solution.py:43
  197.1 0.3 fusion.4
  197.4 48.5 %all-to-all-done.2 = bf16[16,32,16,128]{3,2,1,0:T(8,128)(2,1)S(1)} async-done(((bf16[16,32,16,128]{3,2,1,0:T(8,128)(2,1)}), bf16[16,32,16,128]{3,2,1,0:T(8,128)(2,1)S(1)}, u32[]{:S(2)}, u32[]{:S(2)}) %all-to-all-start.2) | async-done | bytes 2097184 | tf_op jit(solution)/shard_map/all_to_all | solution.py:43
  246.0 0.0 all-gather.2.cloned.1.call-done
  246.0 15.3 %convert_reduce_fusion = (f32[32,16]{1,0:T(8,128)S(1)}, f32[32,16,128]{2,1,0:T(8,128)S(1)}) fusion(bf16[512,16,128]{2,1,0:T(8,128)(2,1)S(1)} %bitcast.34, bf16[512,32,128]{2,1,0:T(8,128)(2,1)} %all-gather.2.cloned.1.call-done), kind=kLoop, calls=%fused_computation | loop fusion | flops 134151680 | bytes 6555648 | tf_op jit(solution)/shard_map/reduce_sum | solution.py:8
  261.3 0.2 multiply_reduce_fusion.2
  261.6 1.0 fusion.10
  (10 shorter events, 0.1 us)
Async XLA Ops:
  12.8 68.7 %all-to-all-start = ((bf16[16,16,32,128]{3,2,1,0:T(8,128)(2,1)}), bf16[16,16,32,128]{3,2,1,0:T(8,128)(2,1)S(1)}, u32[]{:S(2)}, u32[]{:S(2)}) async-start(bf16[16,16,32,128]{3,2,1,0:T(8,128)(2,1)} %stack.2), calls=%async_computation | async-start | bytes 4194304 | tf_op jit(solution)/shard_map/all_to_all | solution.py:69
  24.7 70.1 %copy-start.1 = (bf16[32,16,128]{2,1,0:T(8,128)(2,1)S(1)}, bf16[32,16,128]{2,1,0:T(8,128)(2,1)}, u32[]{:S(2)}) copy-start(bf16[32,16,128]{2,1,0:T(8,128)(2,1)} %param.5) | copy-start | bytes 393220
  24.7 70.1 %copy-start.3 = (bf16[2,128,128]{2,1,0:T(8,128)(2,1)S(1)}, bf16[2,128,128]{2,1,0:T(8,128)(2,1)}, u32[]{:S(2)}) copy-start(bf16[2,128,128]{2,1,0:T(8,128)(2,1)} %param.8) | copy-start | bytes 196612
  24.7 6.7 %collective-permute-start = (bf16[32,16,128]{2,1,0:T(8,128)(2,1)S(1)}, bf16[32,16,128]{2,1,0:T(8,128)(2,1)S(1)}, u32[]{:S(2)}, u32[]{:S(2)}) collective-permute-start(bf16[32,16,128]{2,1,0:T(8,128)(2,1)S(1)} %get-tuple-element.18), channel_id=1, source_target_pairs={{0,0},{2,32},{4,64},{6,96},{8,128},{10,160},{12,192},{14,224},{16,... | collective-permute-start | bytes 393224 | tf_op jit(solution)/shard_map/ppermute | solution.py:38
  83.3 61.7 %all-to-all-start.1 = ((bf16[16,16,32,128]{3,2,1,0:T(8,128)(2,1)}), bf16[16,16,32,128]{3,2,1,0:T(8,128)(2,1)}, u32[]{:S(2)}, u32[]{:S(2)}) async-start(bf16[16,16,32,128]{3,2,1,0:T(8,128)(2,1)} %broadcast_in_dim.4), calls=%async_computation.1 | async-start | bytes 4194304 | tf_op jit(solution)/shard_map/all_to_all | solution.py:43
  94.7 151.2 %all-gather.2.cloned.1.call-start = ((), (), s32[]{:S(2)}) async-start(), calls=%async_computation.3 | async-start | bytes 4456448 | tf_op jit(solution)/shard_map/all_gather | solution.py:94
  145.0 2.8 %copy-start = (f32[256,32,128]{2,1,0:T(8,128)S(1)}, f32[256,32,128]{2,1,0:T(8,128)}, u32[]{:S(2)}) copy-start(f32[256,32,128]{2,1,0:T(8,128)} %bitcast_convert_fusion) | copy-start | bytes 12582916
  154.2 10.6 %copy-start.4 = (bf16[2,128,128]{2,1,0:T(8,128)(2,1)S(1)}, bf16[2,128,128]{2,1,0:T(8,128)(2,1)}, u32[]{:S(2)}) copy-start(bf16[2,128,128]{2,1,0:T(8,128)(2,1)} %param.9) | copy-start | bytes 196612
  154.3 11.3 %copy-start.2 = (bf16[2,128,512]{2,1,0:T(8,128)(2,1)S(1)}, bf16[2,128,512]{2,1,0:T(8,128)(2,1)}, u32[]{:S(2)}) copy-start(bf16[2,128,512]{2,1,0:T(8,128)(2,1)} %param.7) | copy-start | bytes 786436
  154.3 10.1 %collective-permute-start.1 = (bf16[32,16,128]{2,1,0:T(8,128)(2,1)S(1)}, bf16[32,16,128]{2,1,0:T(8,128)(2,1)S(1)}, u32[]{:S(2)}, u32[]{:S(2)}) collective-permute-start(bf16[32,16,128]{2,1,0:T(8,128)(2,1)S(1)} %multiply_reduce_fusion.1), channel_id=1, source_target_pairs={{0,1},{1,0},{2,3},{3,2},{4,5},{5,4},{6,7},{7,6},{8,9},{9,8},{10,11... | collective-permute-start | bytes 393224 | tf_op jit(solution)/shard_map/ppermute | solution.py:85
  166.1 7.5 %collective-permute-start.2 = (bf16[32,16,128]{2,1,0:T(8,128)(2,1)S(1)}, bf16[32,16,128]{2,1,0:T(8,128)(2,1)S(1)}, u32[]{:S(2)}, u32[]{:S(2)}) collective-permute-start(bf16[32,16,128]{2,1,0:T(8,128)(2,1)S(1)} %get-tuple-element.15), channel_id=1, source_target_pairs={{0,0},{2,32},{4,64},{6,96},{8,128},{10,160},{12,192},{14,224},{16,... | collective-permute-start | bytes 393224 | tf_op jit(solution)/shard_map/ppermute | solution.py:38
  173.5 7.2 %collective-permute-start.3 = (bf16[32,16,128]{2,1,0:T(8,128)(2,1)S(1)}, bf16[32,16,128]{2,1,0:T(8,128)(2,1)S(1)}, u32[]{:S(2)}, u32[]{:S(2)}) collective-permute-start(bf16[32,16,128]{2,1,0:T(8,128)(2,1)S(1)} %collective-permute-done.2), channel_id=1, source_target_pairs={{0,1},{1,0},{2,3},{3,2},{4,5},{5,4},{6,7},{7,6},{8,9},{9,8},{10,11... | collective-permute-start | bytes 393224 | tf_op jit(solution)/shard_map/ppermute | solution.py:59
  183.3 62.6 %all-to-all-start.2 = ((bf16[16,32,16,128]{3,2,1,0:T(8,128)(2,1)}), bf16[16,32,16,128]{3,2,1,0:T(8,128)(2,1)S(1)}, u32[]{:S(2)}, u32[]{:S(2)}) async-start(bf16[16,32,16,128]{3,2,1,0:T(8,128)(2,1)} %broadcast_in_dim.5), calls=%async_computation.2 | async-start | bytes 4194304 | tf_op jit(solution)/shard_map/all_to_all | solution.py:43
Sparse Core Ops, SparseCore 0:
  181.7 51.8 all-gather.1
